TPU v7x, 32 devices: a whole 2x2x4 slice. The times are simulated.
32 devices in a mesh: dp: 4 (over y, core), seq: 8 (over z, x).
Axes of the slice: x: 2, y: 2, z: 4, core: 2. Of those that a mesh axis runs over, the one named last changes fastest.
Arguments:
- layer_input: bfloat16 [4, 4096, 1024], P('dp', 'seq'), may hold values from -28 to 28
- w_query: bfloat16 [1024, 1024], replicated, may hold values from -0.1875 to 0.1875
- w_key: bfloat16 [1024, 1024], replicated, may hold values from -0.1875 to 0.1875
- w_value: bfloat16 [1024, 1024], replicated, may hold values from -0.1875 to 0.1875
- w_out: bfloat16 [1024, 1024], replicated, may hold values from -0.1875 to 0.1875
- offsets: int32 [3], replicated, may hold values from 0 to 3
- grad_out: bfloat16 [4, 4096, 1024], P('dp', 'seq'), may hold values from -6 to 6
Outputs:
- layer_output: bfloat16 [4, 4096, 1024], P('dp', 'seq')
- grad_x: bfloat16 [4, 4096, 1024], P('dp', 'seq')
- grad_query: float32 [1024, 1024], P('seq')
- grad_key: float32 [1024, 1024], P('seq')
- grad_value: float32 [1024, 1024], P('seq')
- grad_outw: float32 [1024, 1024], P('seq')
All inputs are finite; a program needn't handle non-finite values.
Results may differ from a plain program's by a relative error of at most 0.018.
The roundings to bfloat16 on the way count: a program that leaves them out, or rounds other values in their place, can miss the bound.
Values may be sent and summed in bfloat16 or wider, within the bound.
No kernel may reach another device: no remote copies, remote signals or barrier semaphores. Data moves between devices by JAX's collectives and lax.ppermute only.
A program may use at most 192 MiB of HBM per device.

v0:
```python
import jax
import jax.numpy as jnp
from jax import lax
from jax.sharding import PartitionSpec as P

HEADS = 16
BLOCK = 128


def partner(array, axis, apart):
    return lax.ppermute(array, axis, [(i, i ^ 1 << apart) for i in range(lax.axis_size(axis))])


def swap_blocks(keys_local, values_local, offsets, levels):
    remote = []
    for level in range(levels):
        start = offsets[level] * BLOCK
        pair = jnp.stack(
            [
                lax.dynamic_slice_in_dim(keys_local, start, BLOCK, 0),
                lax.dynamic_slice_in_dim(values_local, start, BLOCK, 0),
            ]
        )
        remote.append(partner(pair, "seq", level))
    return remote


def gradient_terms(sources):
    parts = []
    for left, right in sources:
        parts.append(jnp.dot(left.T, right, preferred_element_type=jnp.float32))
    return jnp.concatenate(parts, axis=1)


def body(layer_input, w_query, w_key, w_value, w_out, offsets, grad_out):
    rows = layer_input[0]
    cot = grad_out[0]
    tok = rows.shape[0]
    width = rows.shape[1]
    head = width // HEADS
    scale = head ** (-0.5)
    levels = lax.axis_size("seq").bit_length() - 1
    query = jnp.dot(rows, w_query, preferred_element_type=jnp.float32).astype(jnp.bfloat16)
    keys_local = jnp.dot(rows, w_key, preferred_element_type=jnp.float32).astype(jnp.bfloat16)
    values_local = jnp.dot(rows, w_value, preferred_element_type=jnp.float32).astype(jnp.bfloat16)
    remote = swap_blocks(keys_local, values_local, offsets, levels)
    all_keys = jnp.concatenate([keys_local] + [piece[0] for piece in remote], 0)
    all_values = jnp.concatenate([values_local] + [piece[1] for piece in remote], 0)
    total_keys = all_keys.shape[0]
    group = min(tok, 512)
    count = tok // group

    def split3(a):
        return a.reshape(a.shape[0], HEADS, head)

    def forward(query_group):
        scores = (
            jnp.einsum(
                "qhe,khe->hqk",
                split3(query_group),
                split3(all_keys),
                preferred_element_type=jnp.float32,
            )
            * scale
        )
        top = jnp.max(scores, axis=-1, keepdims=True)
        lse = top + jnp.log(jnp.sum(jnp.exp(scores - top), axis=-1, keepdims=True))
        prob_b = jnp.exp(scores - lse).astype(jnp.bfloat16)
        attended = jnp.einsum(
            "hqk,khe->qhe", prob_b, split3(all_values), preferred_element_type=jnp.float32
        )
        return (attended.reshape(group, width).astype(jnp.bfloat16), lse)

    query_groups = query.reshape(count, group, width)
    att_groups, lses = lax.map(forward, query_groups)
    attended = att_groups.reshape(tok, width)
    result = jnp.dot(attended, w_out, preferred_element_type=jnp.float32).astype(jnp.bfloat16)
    d_att = jnp.dot(cot, w_out.T, preferred_element_type=jnp.float32).astype(jnp.bfloat16)

    def backward(carry, item):
        query_group, dgroup, lse = item
        scores = (
            jnp.einsum(
                "qhe,khe->hqk",
                split3(query_group),
                split3(all_keys),
                preferred_element_type=jnp.float32,
            )
            * scale
        )
        prob = jnp.exp(scores - lse)
        prob_b = prob.astype(jnp.bfloat16)
        dprob = jnp.einsum(
            "qhe,khe->hqk", split3(dgroup), split3(all_values), preferred_element_type=jnp.float32
        )
        delta = jnp.sum(prob * dprob, axis=-1, keepdims=True)
        dscore = (prob * (dprob - delta) * scale).astype(jnp.bfloat16)
        dquery = jnp.einsum(
            "hqk,khe->qhe", dscore, split3(all_keys), preferred_element_type=jnp.float32
        )
        dkeys = jnp.einsum(
            "hqk,qhe->khe", dscore, split3(query_group), preferred_element_type=jnp.float32
        )
        dvalues = jnp.einsum(
            "hqk,qhe->khe", prob_b, split3(dgroup), preferred_element_type=jnp.float32
        )
        new_carry = (
            carry[0] + dkeys.reshape(total_keys, width),
            carry[1] + dvalues.reshape(total_keys, width),
        )
        return (new_carry, dquery.reshape(group, width).astype(jnp.bfloat16))

    empty = jnp.zeros((total_keys, width), jnp.float32)
    (dk_acc, dv_acc), dq_groups = lax.scan(
        backward, (empty, empty), (query_groups, d_att.reshape(count, group, width), lses)
    )
    dquery = dq_groups.reshape(tok, width)
    dkey_sum = dk_acc[:tok]
    dvalue_sum = dv_acc[:tok]
    for level in range(levels):
        low = tok + level * BLOCK
        piece = jnp.stack([dk_acc[low : low + BLOCK], dv_acc[low : low + BLOCK]])
        returned = partner(piece.astype(jnp.bfloat16), "seq", level).astype(piece.dtype)
        start = offsets[level] * BLOCK
        dkey_sum = lax.dynamic_update_slice_in_dim(
            dkey_sum, lax.dynamic_slice_in_dim(dkey_sum, start, BLOCK, 0) + returned[0], start, 0
        )
        dvalue_sum = lax.dynamic_update_slice_in_dim(
            dvalue_sum,
            lax.dynamic_slice_in_dim(dvalue_sum, start, BLOCK, 0) + returned[1],
            start,
            0,
        )
    dkey = dkey_sum.astype(jnp.bfloat16)
    dvalue = dvalue_sum.astype(jnp.bfloat16)
    total = jnp.dot(dquery, w_query.T, preferred_element_type=jnp.float32)
    total = total + jnp.dot(dkey, w_key.T, preferred_element_type=jnp.float32)
    total = total + jnp.dot(dvalue, w_value.T, preferred_element_type=jnp.float32)
    grad_input = total.astype(jnp.bfloat16)
    sources = ((rows, dquery), (rows, dkey), (rows, dvalue), (attended, cot))
    part = lax.psum_scatter(
        gradient_terms(sources).astype(jnp.bfloat16), "seq", scatter_dimension=0, tiled=True
    )
    summed = lax.psum(part, "dp").astype(jnp.float32)
    return (
        result[None],
        grad_input[None],
        summed[:, :width],
        summed[:, width : 2 * width],
        summed[:, 2 * width : 3 * width],
        summed[:, 3 * width :],
    )


def solution(mesh):
    return jax.shard_map(
        body,
        mesh=mesh,
        in_specs=(P("dp", "seq", None), P(), P(), P(), P(), P(), P("dp", "seq", None)),
        out_specs=(
            P("dp", "seq", None),
            P("dp", "seq", None),
            P("seq", None),
            P("seq", None),
            P("seq", None),
            P("seq", None),
        ),
        check_vma=False,
    )
```

profile of v0, /device:TPU:0, one launch (start us, length us, event | category | flops | bytes accessed | tf_op | source)
XLA Modules:
  0.0 489.7 jit_solution(11821833035171614596)
XLA Ops:
  10.6 3.3 convolution_convert_fusion.4
  14.0 2.2 convolution_convert_fusion.5
  18.5 3.0 collective-permute-start.1
  22.3 2.6 collective-permute-start.2
  27.3 2.2 convolution_convert_fusion.3
  29.5 2.3 convolution_convert_fusion.1
  31.8 2.8 copy.37
  35.9 2.3 copy.41
  39.7 4.3 collective-permute-done.1
  48.8 1.9 fusion.78
  59.7 15.5 %multiply_reduce_fusion.1 = (f32[16,512]{1,0:T(8,128)S(1)}, f32[16,512,896]{2,1,0:T(8,128)}) fusion(bf16[512,16,64]{0,2,1:T(8,128)(2,1)} %bitcast.130, bf16[128,16,64]{0,2,1:T(8,128)(2,1)} %bitcast.144, bf16[128,16,64]{0,2,1:T(8,128)(2,1)} %bitcast.142, bf16[128,16,64]{0,2,1:T(8,128)(2,1)} %bitcast.146, bf16[512,16,64]{0,2,1:T(8,128)(2,1)} %bitcast.132), kind=kOutput, calls=%fused_computation.6 | convolution fusion | flops 961536000 | bytes 32276480 | tf_op jit(solution)/shard_map/while/body/eval_jaxpr/qhe,khe->hqk/dot_general | solution.py:58
  75.1 13.1 %exponential_reduce_fusion = f32[16,512]{1,0:T(8,128)S(1)} fusion(f32[16,512,896]{2,1,0:T(8,128)} %get-tuple-element.101, f32[16,512]{1,0:T(8,128)S(1)} %get-tuple-element.100), kind=kLoop, calls=%fused_computation.5 | loop fusion | flops 22011904 | bytes 29425664 | tf_op jit(solution)/shard_map/while/body/eval_jaxpr/reduce_sum | solution.py:67
  88.3 11.6 %fusion.60 = f32[16,512,896]{2,1,0:T(8,128)} fusion(bf16[512,16,64]{0,2,1:T(8,128)(2,1)S(1)} %bitcast.125, bf16[128,16,64]{0,2,1:T(8,128)(2,1)S(1)} %bitcast.139, bf16[128,16,64]{0,2,1:T(8,128)(2,1)S(1)} %bitcast.136, bf16[128,16,64]{0,2,1:T(8,128)(2,1)S(1)} %bitcast.141, bf16[512,16,64]{0,2,1:T(8,128)(2,1)S(1)} %bitcast.128), kind=kOutput, calls=%fused_computation.72 | convolution fusion | flops 946864128 | bytes 32243712 | tf_op jit(solution)/shard_map/while/body/eval_jaxpr/qhe,khe->hqk/dot_general | solution.py:93
  100.0 60.6 %fusion.29 = bf16[16,64,512]{2,1,0:T(8,128)(2,1)} fusion(f32[16,512,896]{2,1,0:T(8,128)} %fusion.60, f32[16,512,896]{2,1,0:T(8,128)} %get-tuple-element.101, f32[16,512]{1,0:T(8,128)S(1)} %log_add_fusion, bf16[128,16,64]{0,2,1:T(8,128)(2,1)} %bitcast.145, bf16[128,16,64]{0,2,1:T(8,128)(2,1)} %bitcast.143, bf16[128,16,64]{0,2,1:T(8,128)(2,1)} %bitcast.147, ...), kind=kOutput, calls=%fused_computation.31 | convolution fusion | flops 1013457792 | bytes 61636608 | tf_op jit(solution)/shard_map/while/body/eval_jaxpr/hqk,khe->qhe/dot_general | solution.py:98
  160.6 54.9 %fusion.81 = (bf16[896,16,64]{0,2,1:T(8,128)(2,1)}, f32[896,16,64]{0,2,1:T(8,128)}) fusion(bf16[512,16,64]{0,2,1:T(8,128)(2,1)} %bitcast.131, f32[16,512,896]{2,1,0:T(8,128)} %fusion.60, f32[16,512,896]{2,1,0:T(8,128)} %get-tuple-element.101, f32[16,512]{1,0:T(8,128)S(1)} %log_add_fusion), kind=kOutput, calls=%fused_computation.98 | convolution fusion | flops 1006510976 | bytes 65306624 | tf_op jit(solution)/shard_map/while/body/eval_jaxpr/hqk,qhe->khe/dot_general | solution.py:101
  215.5 13.6 %fusion.26 = bf16[16,64,512]{2,1,0:T(8,128)(2,1)} fusion(f32[16,512,896]{2,1,0:T(8,128)} %get-tuple-element.101, f32[16,512]{1,0:T(8,128)S(1)} %log_add_fusion, bf16[128,16,64]{0,2,1:T(8,128)(2,1)} %bitcast.138, bf16[128,16,64]{0,2,1:T(8,128)(2,1)S(1)} %bitcast.137, bf16[128,16,64]{0,2,1:T(8,128)(2,1)} %bitcast.140, bf16[512,16,64]{0,2,1:T(8,128)(2,1)} %bitcast.127), kind=kOutput, calls=%fused_computation.25 | convolution fusion | flops 969408512 | bytes 32276480 | tf_op jit(solution)/shard_map/while/body/eval_jaxpr/hqk,khe->qhe/dot_general | solution.py:69
  229.1 11.7 %fusion.80 = (bf16[896,16,64]{0,2,1:T(8,128)(2,1)S(1)}, f32[896,16,64]{0,2,1:T(8,128)S(1)}) fusion(bf16[512,16,64]{0,2,1:T(8,128)(2,1)S(1)} %bitcast.126, f32[16,512,896]{2,1,0:T(8,128)} %get-tuple-element.101, f32[16,512]{1,0:T(8,128)S(1)} %log_add_fusion), kind=kOutput, calls=%fused_computation.97 | convolution fusion | flops 962461696 | bytes 35946496 | tf_op jit(solution)/shard_map/while/body/eval_jaxpr/hqk,qhe->khe/dot_general | solution.py:104
  244.4 3.1 collective-permute-start.5
  251.9 3.8 collective-permute-done.3
  255.7 12.0 %collective-permute-done.4 = bf16[2,128,1024]{1,2,0:T(8,128)(2,1)S(1)} collective-permute-done((bf16[2,128,1024]{1,2,0:T(8,128)(2,1)S(1)}, bf16[2,128,1024]{1,2,0:T(8,128)(2,1)S(1)}, u32[]{:S(2)}, u32[]{:S(2)}) %collective-permute-start.4) | collective-permute-done | bytes 524320 | tf_op jit(solution)/shard_map/ppermute | solution.py:11
  272.9 4.0 pad_maximum_fusion
  276.9 11.5 %copy.51 = bf16[1024,4096]{1,0:T(8,128)(2,1)} copy(bf16[1024,4096]{0,1:T(8,128)(2,1)} %pad_maximum_fusion) | data formatting | bytes 16777216
  288.5 2.2 fusion.32
  290.8 2.7 fusion.84
  293.5 2.7 fusion.57
  296.2 140.5 %reduce-scatter.4.cloned.1.call-done = bf16[128,4096]{1,0:T(8,128)(2,1)} async-done(((bf16[1024,4096]{1,0:T(8,128)(2,1)}), bf16[128,4096]{1,0:T(8,128)(2,1)}) %reduce-scatter.4.cloned.1.call-update) | async-done | bytes 1048592
  436.7 2.3 copy.52
  439.0 5.8 %fusion.33 = bf16[1,512,1024]{2,1,0:T(8,128)(2,1)} fusion(bf16[1024,1024]{1,0:T(8,128)(2,1)} %param.10, f32[512,1024]{1,0:T(8,128)} %fusion.84, f32[512,1024]{1,0:T(8,128)} %fusion.57, f32[512,1024]{0,1:T(8,128)} %copy-done.1), kind=kOutput, calls=%fused_computation.33 | convolution fusion | flops 1075838976 | bytes 9437184 | tf_op jit(solution)/shard_map/dot_general | solution.py:138
  444.8 29.6 %all-reduce.2.cloned.1.call-done = bf16[128,4096]{0,1:T(8,128)(2,1)} async-done(((bf16[128,4096]{0,1:T(8,128)(2,1)}), bf16[128,4096]{0,1:T(8,128)(2,1)}) %all-reduce.2.cloned.1.call-update) | async-done | bytes 1048592 | tf_op jit(solution)/shard_map/psum | solution.py:144
  474.3 2.3 fusion.75
  476.6 2.0 copy.50
  478.7 2.0 copy.49
  (85 shorter events, 38.7 us)
Async XLA Ops:
  7.2 22.3 %copy-start = (bf16[1024,1024]{1,0:T(8,128)(2,1)S(1)}, bf16[1024,1024]{1,0:T(8,128)(2,1)}, u32[]{:S(2)}) copy-start(bf16[1024,1024]{1,0:T(8,128)(2,1)} %param.11) | copy-start | bytes 6291460
  7.2 429.5 %reduce-scatter.4.cloned.1.call-start = ((), (), s32[]{:S(2)}) async-start(), calls=%async_computation.2 | async-start | bytes 9437184
  10.6 3.3 copy-start.8
  10.6 3.3 copy-start.15
  16.2 11.1 %copy-start.10 = (bf16[1024,1024]{1,0:T(8,128)(2,1)S(1)}, bf16[1024,1024]{1,0:T(8,128)(2,1)}, u32[]{:S(2)}) copy-start(bf16[1024,1024]{1,0:T(8,128)(2,1)} %param.8) | copy-start | bytes 6291460
  16.2 11.1 %copy-start.16 = (bf16[1,512,1024]{2,1,0:T(8,128)(2,1)S(1)}, bf16[1,512,1024]{2,1,0:T(8,128)(2,1)}, u32[]{:S(2)}) copy-start(bf16[1,512,1024]{2,1,0:T(8,128)(2,1)} %param.7) | copy-start | bytes 3145732
  18.5 25.5 %collective-permute-start.1 = (bf16[2,128,1024]{2,1,0:T(8,128)(2,1)}, bf16[2,128,1024]{2,1,0:T(8,128)(2,1)}, u32[]{:S(2)}, u32[]{:S(2)}) collective-permute-start(bf16[2,128,1024]{2,1,0:T(8,128)(2,1)} %pad_maximum_fusion.4), channel_id=1, source_target_pairs={{0,2},{1,3},{2,0},{3,1},{4,6},{5,7},{6,4},{7,5},{8,10},{9,11},{10,... | collective-permute-start | bytes 1572872 | tf_op jit(solution)/shard_map/ppermute | solution.py:11
  22.3 26.5 %collective-permute-start.2 = (bf16[2,128,1024]{2,1,0:T(8,128)(2,1)}, bf16[2,128,1024]{2,1,0:T(8,128)(2,1)}, u32[]{:S(2)}, u32[]{:S(2)}) collective-permute-start(bf16[2,128,1024]{2,1,0:T(8,128)(2,1)} %pad_maximum_fusion.5), channel_id=1, source_target_pairs={{0,4},{1,5},{2,6},{3,7},{4,0},{5,1},{6,2},{7,3},{8,12},{9,13},{10,... | collective-permute-start | bytes 1572872 | tf_op jit(solution)/shard_map/ppermute | solution.py:11
  25.8 3.7 copy-start.13
  25.8 28.5 %collective-permute-start = (bf16[2,128,1024]{2,1,0:T(8,128)(2,1)}, bf16[2,128,1024]{2,1,0:T(8,128)(2,1)}, u32[]{:S(2)}, u32[]{:S(2)}) collective-permute-start(bf16[2,128,1024]{2,1,0:T(8,128)(2,1)} %pad_maximum_fusion.3), channel_id=1, source_target_pairs={{0,1},{1,0},{2,3},{3,2},{4,5},{5,4},{6,7},{7,6},{8,9},{9,8},{10,11... | collective-permute-start | bytes 1572872 | tf_op jit(solution)/shard_map/ppermute | solution.py:11
  75.1 13.2 %copy-start.2 = (bf16[512,1024]{0,1:T(8,128)(2,1)S(1)}, bf16[512,1024]{0,1:T(8,128)(2,1)}, u32[]{:S(2)}) copy-start(bf16[512,1024]{0,1:T(8,128)(2,1)} %copy.37) | copy-start | bytes 3145732
  75.1 13.2 %copy-start.6 = (bf16[1,128,1024]{1,2,0:T(8,128)(2,1)S(1)}, bf16[1,128,1024]{1,2,0:T(8,128)(2,1)}, u32[]{:S(2)}) copy-start(bf16[1,128,1024]{1,2,0:T(8,128)(2,1)} %copy.40) | copy-start | bytes 786436
  75.1 13.2 %copy-start.7 = (bf16[1,128,1024]{1,2,0:T(8,128)(2,1)S(1)}, bf16[1,128,1024]{1,2,0:T(8,128)(2,1)}, u32[]{:S(2)}) copy-start(bf16[1,128,1024]{1,2,0:T(8,128)(2,1)} %copy.38) | copy-start | bytes 786436
  240.9 6.6 %copy-start.9 = (f32[896,16,64]{0,2,1:T(8,128)S(1)}, f32[896,16,64]{0,2,1:T(8,128)}, u32[]{:S(2)}) copy-start(f32[896,16,64]{0,2,1:T(8,128)} %get-tuple-element.105) | copy-start | bytes 11010052
  242.5 13.2 %collective-permute-start.3 = (bf16[2,128,1024]{1,2,0:T(8,128)(2,1)S(1)}, bf16[2,128,1024]{1,2,0:T(8,128)(2,1)S(1)}, u32[]{:S(2)}, u32[]{:S(2)}) collective-permute-start(bf16[2,128,1024]{1,2,0:T(8,128)(2,1)S(1)} %pad_maximum_fusion.6), channel_id=1, source_target_pairs={{0,1},{1,0},{2,3},{3,2},{4,5},{5,4},{6,7},{7,6},{8,9},{9,8},{10,11... | collective-permute-start | bytes 1572872 | tf_op jit(solution)/shard_map/ppermute | solution.py:11
  244.3 23.5 %collective-permute-start.4 = (bf16[2,128,1024]{1,2,0:T(8,128)(2,1)S(1)}, bf16[2,128,1024]{1,2,0:T(8,128)(2,1)S(1)}, u32[]{:S(2)}, u32[]{:S(2)}) collective-permute-start(bf16[2,128,1024]{1,2,0:T(8,128)(2,1)S(1)} %pad_maximum_fusion.7), channel_id=1, source_target_pairs={{0,2},{1,3},{2,0},{3,1},{4,6},{5,7},{6,4},{7,5},{8,10},{9,11},{10,... | collective-permute-start | bytes 1572872 | tf_op jit(solution)/shard_map/ppermute | solution.py:11
  244.4 24.9 %collective-permute-start.5 = (bf16[2,128,1024]{1,2,0:T(8,128)(2,1)S(1)}, bf16[2,128,1024]{1,2,0:T(8,128)(2,1)S(1)}, u32[]{:S(2)}, u32[]{:S(2)}) collective-permute-start(bf16[2,128,1024]{1,2,0:T(8,128)(2,1)S(1)} %pad_maximum_fusion.8), channel_id=1, source_target_pairs={{0,4},{1,5},{2,6},{3,7},{4,0},{5,1},{6,2},{7,3},{8,12},{9,13},{10,... | collective-permute-start | bytes 1572872 | tf_op jit(solution)/shard_map/ppermute | solution.py:11
  247.5 1.2 copy-start.5
  247.5 1.6 copy-start.14
  249.1 1.3 copy-start.17
  249.1 1.5 copy-start.18
  269.7 1.3 copy-start.1
  269.7 1.9 copy-start.3
  288.5 185.9 %all-reduce.2.cloned.1.call-start = ((), (), s32[]{:S(2)}) async-start(), calls=%async_computation.1 | async-start | bytes 2097152 | tf_op jit(solution)/shard_map/psum | solution.py:144
  288.5 2.3 copy-start.11
  288.5 2.3 copy-start.19
  290.8 2.7 copy-start.4
  290.8 2.7 copy-start.12
Sparse Core Ops, SparseCore 0:
  288.6 148.0 reduce-scatter.3
  439.2 35.1 all-reduce.1
where the time goes:
time: 495 us; the launch traced here: 490 us
  matrix products  197 us (40%)
  waiting for transfers between devices  191 us (39%)
  local copies, waits for them, and re-layouts  52.5 us (11%)
  other arithmetic  21 us (4%)
  between operations  16.5 us (3%)
  starting transfers between devices  12.1 us (2%)
    unnamed x3, waiting for transfers between devices  141 us
    dot_general x1, matrix products, backward(): jnp.einsum('hqk,khe->qhe', dscore, split3(all_keys), preferred_element_ty...  60.6 us
    dot_general x1, matrix products, backward(): jnp.einsum('hqk,qhe->khe', dscore, split3(query_group), preferred_element...  54.9 us
    psum x1, waiting for transfers between devices, body(): summed = lax.psum(part, 'dp').astype(jnp.float32)  29.6 us
    unnamed x46, local copies, waits for them, and re-layouts  21.9 us
    ppermute x6, waiting for transfers between devices, partner(): lax.ppermute(array, axis, [(i, i ^ 1 << apart) for i in range(lax.axis_si...  20.9 us
    dot_general x1, matrix products, forward(): jnp.einsum('qhe,khe->hqk', split3(query_group), split3(all_keys), preferr...  15.5 us
    dot_general x1, matrix products, forward(): jnp.einsum('hqk,khe->qhe', prob_b, split3(all_values), preferred_element_...  13.6 us
  transfers between devices with their start and end apart: 8, of which 6 were waited for; matrix products, arithmetic and copies ran while one was open for 8% of the time, Pallas kernels for 0%

commit v1 on v0

--- a/solution.py
+++ b/solution.py
@@ -5,6 +5,11 @@
 
 HEADS = 16
 BLOCK = 128
+
+
+def gather_and_add(value, mesh_axis):
+    parts = lax.all_gather(value, mesh_axis)
+    return jnp.sum(parts, axis=0)
 
 
 def partner(array, axis, apart):
@@ -141,7 +146,7 @@
     part = lax.psum_scatter(
         gradient_terms(sources).astype(jnp.bfloat16), "seq", scatter_dimension=0, tiled=True
     )
-    summed = lax.psum(part, "dp").astype(jnp.float32)
+    summed = gather_and_add(part, "dp").astype(jnp.float32)
     return (
         result[None],
         grad_input[None],

time: 495 us -> 525 us (1.061)
  other arithmetic: 21 us -> 44 us
  local copies, waits for them, and re-layouts: 52.5 us -> 62.8 us
  matrix products: 197 us -> 191 us
    psum x1 -> x0, waiting for transfers between devices: 29.6 us -> none  [body(): summed = lax.psum(part, 'dp').astype(jnp.float32)]
    all_gather x0 -> x1, waiting for transfers between devices: none -> 24.7 us  [gather_and_add(): parts = lax.all_gather(value, mesh_axis)]
    reduce_sum x0 -> x1, other arithmetic: none -> 23 us  [gather_and_add(): return jnp.sum(parts, axis=0)]
    unnamed x3, waiting for transfers between devices: 141 us -> 148 us
    all_gather x0 -> x1, local copies, waits for them, and re-layouts: none -> 6.97 us  [gather_and_add(): parts = lax.all_gather(value, mesh_axis)]
    unnamed x46 -> x50, local copies, waits for them, and re-layouts: 21.9 us -> 26.3 us
  transfers between devices with their start and end apart: 8 -> 8, of which waited for: 6 -> 6; matrix products, arithmetic and copies ran while one was open for 8% -> 7% of each run, Pallas kernels for 0% -> 0%
where the time goes in v1:
time: 525 us; the launch traced here: 520 us
  waiting for transfers between devices  194 us (37%)
  matrix products  191 us (36%)
  local copies, waits for them, and re-layouts  62.8 us (12%)
  other arithmetic  44 us (8%)
  between operations  16.6 us (3%)
  starting transfers between devices  12.1 us (2%)
    unnamed x3, waiting for transfers between devices  148 us
    dot_general x1, matrix products, backward(): jnp.einsum('hqk,khe->qhe', dscore, split3(all_keys), preferred_element_ty...  60.9 us
    dot_general x1, matrix products, backward(): jnp.einsum('hqk,qhe->khe', dscore, split3(query_group), preferred_element...  55 us
    unnamed x50, local copies, waits for them, and re-layouts  26.3 us
    all_gather x1, waiting for transfers between devices, gather_and_add(): parts = lax.all_gather(value, mesh_axis)  24.7 us
    reduce_sum x1, other arithmetic, gather_and_add(): return jnp.sum(parts, axis=0)  23 us
    ppermute x6, waiting for transfers between devices, partner(): lax.ppermute(array, axis, [(i, i ^ 1 << apart) for i in range(lax.axis_si...  21.1 us
    dot_general x1, matrix products, forward(): jnp.einsum('qhe,khe->hqk', split3(query_group), split3(all_keys), preferr...  15.5 us
  transfers between devices with their start and end apart: 8, of which 6 were waited for; matrix products, arithmetic and copies ran while one was open for 7% of the time, Pallas kernels for 0%

profile of v1, /device:TPU:0, one launch (start us, length us, event | category | flops | bytes accessed | tf_op | source)
XLA Modules:
  0.0 520.2 jit_solution(4515256450750933415)
XLA Ops:
  10.6 3.3 convolution_convert_fusion.4
  14.0 2.2 convolution_convert_fusion.5
  18.5 3.0 collective-permute-start.1
  22.3 2.6 collective-permute-start.2
  27.3 2.2 convolution_convert_fusion.3
  29.5 2.3 convolution_convert_fusion.1
  31.8 2.6 copy.29
  35.7 2.3 copy.33
  39.5 4.5 collective-permute-done.1
  59.6 15.5 %multiply_reduce_fusion.1 = (f32[16,512]{1,0:T(8,128)S(1)}, f32[16,512,896]{2,1,0:T(8,128)}) fusion(bf16[512,16,64]{0,2,1:T(8,128)(2,1)} %bitcast.132, bf16[128,16,64]{0,2,1:T(8,128)(2,1)} %bitcast.146, bf16[128,16,64]{0,2,1:T(8,128)(2,1)} %bitcast.144, bf16[128,16,64]{0,2,1:T(8,128)(2,1)} %bitcast.148, bf16[512,16,64]{0,2,1:T(8,128)(2,1)} %bitcast.134), kind=kOutput, calls=%fused_computation.6 | convolution fusion | flops 961536000 | bytes 32276480 | tf_op jit(solution)/shard_map/while/body/eval_jaxpr/qhe,khe->hqk/dot_general | solution.py:63
  75.1 13.1 %exponential_reduce_fusion = f32[16,512]{1,0:T(8,128)S(1)} fusion(f32[16,512,896]{2,1,0:T(8,128)} %get-tuple-element.89, f32[16,512]{1,0:T(8,128)S(1)} %get-tuple-element.88), kind=kLoop, calls=%fused_computation.5 | loop fusion | flops 22011904 | bytes 29425664 | tf_op jit(solution)/shard_map/while/body/eval_jaxpr/reduce_sum | solution.py:72
  88.3 11.6 %fusion.60 = f32[16,512,896]{2,1,0:T(8,128)} fusion(bf16[512,16,64]{0,2,1:T(8,128)(2,1)S(1)} %bitcast.127, bf16[128,16,64]{0,2,1:T(8,128)(2,1)S(1)} %bitcast.141, bf16[128,16,64]{0,2,1:T(8,128)(2,1)S(1)} %bitcast.138, bf16[128,16,64]{0,2,1:T(8,128)(2,1)S(1)} %bitcast.143, bf16[512,16,64]{0,2,1:T(8,128)(2,1)S(1)} %bitcast.130), kind=kOutput, calls=%fused_computation.72 | convolution fusion | flops 946864128 | bytes 32243712 | tf_op jit(solution)/shard_map/while/body/eval_jaxpr/qhe,khe->hqk/dot_general | solution.py:98
  100.0 60.9 %fusion.29 = bf16[16,64,512]{2,1,0:T(8,128)(2,1)} fusion(f32[16,512,896]{2,1,0:T(8,128)} %fusion.60, f32[16,512,896]{2,1,0:T(8,128)} %get-tuple-element.89, f32[16,512]{1,0:T(8,128)S(1)} %log_add_fusion, bf16[128,16,64]{0,2,1:T(8,128)(2,1)} %bitcast.147, bf16[128,16,64]{0,2,1:T(8,128)(2,1)} %bitcast.145, bf16[128,16,64]{0,2,1:T(8,128)(2,1)} %bitcast.149, ...), kind=kOutput, calls=%fused_computation.31 | convolution fusion | flops 1013457792 | bytes 61636608 | tf_op jit(solution)/shard_map/while/body/eval_jaxpr/hqk,khe->qhe/dot_general | solution.py:103
  160.9 55.0 %fusion.81 = (bf16[896,16,64]{0,2,1:T(8,128)(2,1)}, f32[896,16,64]{0,2,1:T(8,128)}) fusion(bf16[512,16,64]{0,2,1:T(8,128)(2,1)} %bitcast.133, f32[16,512,896]{2,1,0:T(8,128)} %fusion.60, f32[16,512,896]{2,1,0:T(8,128)} %get-tuple-element.89, f32[16,512]{1,0:T(8,128)S(1)} %log_add_fusion), kind=kOutput, calls=%fused_computation.98 | convolution fusion | flops 1006510976 | bytes 65306624 | tf_op jit(solution)/shard_map/while/body/eval_jaxpr/hqk,qhe->khe/dot_general | solution.py:106
  216.0 13.6 %fusion.26 = bf16[16,64,512]{2,1,0:T(8,128)(2,1)} fusion(f32[16,512,896]{2,1,0:T(8,128)} %get-tuple-element.89, f32[16,512]{1,0:T(8,128)S(1)} %log_add_fusion, bf16[128,16,64]{0,2,1:T(8,128)(2,1)} %bitcast.140, bf16[128,16,64]{0,2,1:T(8,128)(2,1)S(1)} %bitcast.139, bf16[128,16,64]{0,2,1:T(8,128)(2,1)} %bitcast.142, bf16[512,16,64]{0,2,1:T(8,128)(2,1)} %bitcast.129), kind=kOutput, calls=%fused_computation.25 | convolution fusion | flops 969408512 | bytes 32276480 | tf_op jit(solution)/shard_map/while/body/eval_jaxpr/hqk,khe->qhe/dot_general | solution.py:74
  229.6 11.7 %fusion.80 = (bf16[896,16,64]{0,2,1:T(8,128)(2,1)S(1)}, f32[896,16,64]{0,2,1:T(8,128)S(1)}) fusion(bf16[512,16,64]{0,2,1:T(8,128)(2,1)S(1)} %bitcast.128, f32[16,512,896]{2,1,0:T(8,128)} %get-tuple-element.89, f32[16,512]{1,0:T(8,128)S(1)} %log_add_fusion), kind=kOutput, calls=%fused_computation.97 | convolution fusion | flops 962461696 | bytes 35946496 | tf_op jit(solution)/shard_map/while/body/eval_jaxpr/hqk,qhe->khe/dot_general | solution.py:109
  244.8 3.1 collective-permute-start.5
  252.3 3.8 collective-permute-done.3
  256.2 12.0 %collective-permute-done.4 = bf16[2,128,1024]{1,2,0:T(8,128)(2,1)S(1)} collective-permute-done((bf16[2,128,1024]{1,2,0:T(8,128)(2,1)S(1)}, bf16[2,128,1024]{1,2,0:T(8,128)(2,1)S(1)}, u32[]{:S(2)}, u32[]{:S(2)}) %collective-permute-start.4) | collective-permute-done | bytes 524320 | tf_op jit(solution)/shard_map/ppermute | solution.py:16
  273.3 4.0 pad_maximum_fusion
  277.4 11.4 %copy.43 = bf16[1024,4096]{1,0:T(8,128)(2,1)} copy(bf16[1024,4096]{0,1:T(8,128)(2,1)} %pad_maximum_fusion) | data formatting | bytes 16777216
  288.8 148.2 %reduce-scatter.4.cloned.1.call-done = bf16[128,4096]{1,0:T(8,128)(2,1)} async-done(((bf16[1024,4096]{1,0:T(8,128)(2,1)}), bf16[128,4096]{1,0:T(8,128)(2,1)}) %reduce-scatter.4.cloned.1.call-update) | async-done | bytes 1048592
  437.1 2.5 copy.44
  439.6 2.2 fusion.32
  446.7 2.3 fusion.33
  449.0 24.7 %all-gather.3.cloned.1.call-done = bf16[512,4096]{0,1:T(8,128)(2,1)} async-done(((bf16[128,4096]{0,1:T(8,128)(2,1)}), bf16[512,4096]{0,1:T(8,128)(2,1)}) %all-gather.3.cloned.1.call-update) | async-done | bytes 4194320 | tf_op jit(solution)/shard_map/all_gather | solution.py:11
  473.7 7.0 %reshape.105 = bf16[4,128,4096]{1,0,2:T(4,128)(2,1)} reshape(bf16[512,4096]{0,1:T(8,128)(2,1)} %all-gather.3.cloned.1.call-done) | data formatting | bytes 8388608 | tf_op jit(solution)/shard_map/all_gather | solution.py:11
  480.7 23.0 %reduce_sum.34 = bf16[128,4096]{0,1:T(8,128)(2,1)S(1)} reduce(bf16[4,128,4096]{1,0,2:T(4,128)(2,1)} %reshape.105, bf16[]{:T(256)} %constant.46.clone.1), dimensions={0}, to_apply=%region_4.5 | reduce | flops 1572864 | bytes 5242882 | tf_op jit(solution)/shard_map/reduce_sum | solution.py:12
  505.0 2.0 copy.42
  507.1 2.0 copy.41
  509.1 2.0 copy.40
  511.1 2.0 copy.39
  (91 shorter events, 44.7 us)
Async XLA Ops:
  7.2 22.3 %copy-start = (bf16[1024,1024]{1,0:T(8,128)(2,1)S(1)}, bf16[1024,1024]{1,0:T(8,128)(2,1)}, u32[]{:S(2)}) copy-start(bf16[1024,1024]{1,0:T(8,128)(2,1)} %param.11) | copy-start | bytes 6291460
  7.2 429.9 %reduce-scatter.4.cloned.1.call-start = ((), (), s32[]{:S(2)}) async-start(), calls=%async_computation.2 | async-start | bytes 9437184
  10.6 3.3 copy-start.9
  10.6 3.3 copy-start.17
  16.2 11.1 %copy-start.12 = (bf16[1024,1024]{1,0:T(8,128)(2,1)S(1)}, bf16[1024,1024]{1,0:T(8,128)(2,1)}, u32[]{:S(2)}) copy-start(bf16[1024,1024]{1,0:T(8,128)(2,1)} %param.8) | copy-start | bytes 6291460
  16.2 11.1 %copy-start.18 = (bf16[1,512,1024]{2,1,0:T(8,128)(2,1)S(1)}, bf16[1,512,1024]{2,1,0:T(8,128)(2,1)}, u32[]{:S(2)}) copy-start(bf16[1,512,1024]{2,1,0:T(8,128)(2,1)} %param.7) | copy-start | bytes 3145732
  18.5 25.5 %collective-permute-start.1 = (bf16[2,128,1024]{2,1,0:T(8,128)(2,1)}, bf16[2,128,1024]{2,1,0:T(8,128)(2,1)}, u32[]{:S(2)}, u32[]{:S(2)}) collective-permute-start(bf16[2,128,1024]{2,1,0:T(8,128)(2,1)} %pad_maximum_fusion.4), channel_id=1, source_target_pairs={{0,2},{1,3},{2,0},{3,1},{4,6},{5,7},{6,4},{7,5},{8,10},{9,11},{10,... | collective-permute-start | bytes 1572872 | tf_op jit(solution)/shard_map/ppermute | solution.py:16
  22.3 26.5 %collective-permute-start.2 = (bf16[2,128,1024]{2,1,0:T(8,128)(2,1)}, bf16[2,128,1024]{2,1,0:T(8,128)(2,1)}, u32[]{:S(2)}, u32[]{:S(2)}) collective-permute-start(bf16[2,128,1024]{2,1,0:T(8,128)(2,1)} %pad_maximum_fusion.5), channel_id=1, source_target_pairs={{0,4},{1,5},{2,6},{3,7},{4,0},{5,1},{6,2},{7,3},{8,12},{9,13},{10,... | collective-permute-start | bytes 1572872 | tf_op jit(solution)/shard_map/ppermute | solution.py:16
  25.8 3.7 copy-start.15
  25.8 28.5 %collective-permute-start = (bf16[2,128,1024]{2,1,0:T(8,128)(2,1)}, bf16[2,128,1024]{2,1,0:T(8,128)(2,1)}, u32[]{:S(2)}, u32[]{:S(2)}) collective-permute-start(bf16[2,128,1024]{2,1,0:T(8,128)(2,1)} %pad_maximum_fusion.3), channel_id=1, source_target_pairs={{0,1},{1,0},{2,3},{3,2},{4,5},{5,4},{6,7},{7,6},{8,9},{9,8},{10,11... | collective-permute-start | bytes 1572872 | tf_op jit(solution)/shard_map/ppermute | solution.py:16
  75.1 13.2 %copy-start.3 = (bf16[512,1024]{0,1:T(8,128)(2,1)S(1)}, bf16[512,1024]{0,1:T(8,128)(2,1)}, u32[]{:S(2)}) copy-start(bf16[512,1024]{0,1:T(8,128)(2,1)} %copy.29) | copy-start | bytes 3145732
  75.1 13.2 %copy-start.7 = (bf16[1,128,1024]{1,2,0:T(8,128)(2,1)S(1)}, bf16[1,128,1024]{1,2,0:T(8,128)(2,1)}, u32[]{:S(2)}) copy-start(bf16[1,128,1024]{1,2,0:T(8,128)(2,1)} %copy.32) | copy-start | bytes 786436
  75.1 13.2 %copy-start.8 = (bf16[1,128,1024]{1,2,0:T(8,128)(2,1)S(1)}, bf16[1,128,1024]{1,2,0:T(8,128)(2,1)}, u32[]{:S(2)}) copy-start(bf16[1,128,1024]{1,2,0:T(8,128)(2,1)} %copy.30) | copy-start | bytes 786436
  241.3 6.6 %copy-start.11 = (f32[896,16,64]{0,2,1:T(8,128)S(1)}, f32[896,16,64]{0,2,1:T(8,128)}, u32[]{:S(2)}) copy-start(f32[896,16,64]{0,2,1:T(8,128)} %get-tuple-element.93) | copy-start | bytes 11010052
  242.9 13.2 %collective-permute-start.3 = (bf16[2,128,1024]{1,2,0:T(8,128)(2,1)S(1)}, bf16[2,128,1024]{1,2,0:T(8,128)(2,1)S(1)}, u32[]{:S(2)}, u32[]{:S(2)}) collective-permute-start(bf16[2,128,1024]{1,2,0:T(8,128)(2,1)S(1)} %pad_maximum_fusion.6), channel_id=1, source_target_pairs={{0,1},{1,0},{2,3},{3,2},{4,5},{5,4},{6,7},{7,6},{8,9},{9,8},{10,11... | collective-permute-start | bytes 1572872 | tf_op jit(solution)/shard_map/ppermute | solution.py:16
  244.7 23.5 %collective-permute-start.4 = (bf16[2,128,1024]{1,2,0:T(8,128)(2,1)S(1)}, bf16[2,128,1024]{1,2,0:T(8,128)(2,1)S(1)}, u32[]{:S(2)}, u32[]{:S(2)}) collective-permute-start(bf16[2,128,1024]{1,2,0:T(8,128)(2,1)S(1)} %pad_maximum_fusion.7), channel_id=1, source_target_pairs={{0,2},{1,3},{2,0},{3,1},{4,6},{5,7},{6,4},{7,5},{8,10},{9,11},{10,... | collective-permute-start | bytes 1572872 | tf_op jit(solution)/shard_map/ppermute | solution.py:16
  244.8 24.9 %collective-permute-start.5 = (bf16[2,128,1024]{1,2,0:T(8,128)(2,1)S(1)}, bf16[2,128,1024]{1,2,0:T(8,128)(2,1)S(1)}, u32[]{:S(2)}, u32[]{:S(2)}) collective-permute-start(bf16[2,128,1024]{1,2,0:T(8,128)(2,1)S(1)} %pad_maximum_fusion.8), channel_id=1, source_target_pairs={{0,4},{1,5},{2,6},{3,7},{4,0},{5,1},{6,2},{7,3},{8,12},{9,13},{10,... | collective-permute-start | bytes 1572872 | tf_op jit(solution)/shard_map/ppermute | solution.py:16
  247.9 1.2 copy-start.6
  247.9 1.6 copy-start.16
  249.5 1.3 copy-start.19
  249.5 1.5 copy-start.20
  270.1 1.4 copy-start.1
  270.1 1.9 copy-start.4
  288.8 185.0 %all-gather.3.cloned.1.call-start = ((), (), s32[]{:S(2)}) async-start(), calls=%async_computation.1 | async-start | bytes 5242880 | tf_op jit(solution)/shard_map/all_gather | solution.py:11
  439.6 2.3 copy-start.13
  439.6 2.3 copy-start.21
  441.8 1.6 copy-start.5
  441.8 2.2 copy-start.14
  444.0 1.8 copy-start.2
  444.0 2.6 copy-start.10
Sparse Core Ops, SparseCore 0:
  288.9 148.1 reduce-scatter.3
  439.7 34.0 all-gather.2
